TPU v7x, 128 devices: a whole 4x4x4 slice. The times are simulated.
128 devices in a mesh: fsdp: 32 (over y, z, core), seq: 4 (over x).
Axes of the slice: x: 4, y: 4, z: 4, core: 2. Of those that a mesh axis runs over, the one named last changes fastest.
Arguments:
- draft_tokens: bfloat16 [32768, 2048], P('fsdp'), may hold values from -6 to 6
- draft_gate: bfloat16 [2048, 4096], P('fsdp', 'seq'), may hold values from -0.125 to 0.125
- draft_up: bfloat16 [2048, 4096], P('fsdp', 'seq'), may hold values from -0.125 to 0.125
- draft_head: float32 [4096], P('seq'), may hold values from -0.75 to 0.75
- verifier_rows: bfloat16 [32768, 8192], P(('fsdp', 'seq')), may hold values from -6 to 6
- norm_gain: float32 [8192], replicated, may hold values from 0.5 to 1.5
- key_weight: bfloat16 [8192, 512], P('fsdp'), may hold values from -0.06629126 to 0.06629126
- value_weight: bfloat16 [8192, 512], P('fsdp'), may hold values from -0.0625 to 0.0625
- pool_query: float32 [4, 4, 128], replicated, may hold values from -32 to 32
- flags: int32 [1024], P(('fsdp', 'seq')), may hold values from 0 to 1, as said below
- owner: int32 [1024], P(('fsdp', 'seq')), may hold values from 0 to 3
Outputs:
- draft_score: float32 [1024], P(('fsdp', 'seq'))
- verdict: bfloat16 [1024, 512], P(('fsdp', 'seq'))
Inputs may be any that keep to these rules, and one draw needn't show every extreme that they name: `flags`: on the 8 segments of one device, at most 4 flagged segments share an owner lane, and on every device exactly 4 flagged segments share one lane.
All inputs are finite; a program needn't handle non-finite values.
Results may differ from a plain program's by a relative error of at most 0.009.
Values may be sent and summed in bfloat16 or wider, within the bound.
No kernel may reach another device: no remote copies, remote signals or barrier semaphores. Data moves between devices by JAX's collectives and lax.ppermute only.
A program may use at most 128 MiB of HBM per device.

v0:
```python
import math
import jax
import jax.numpy as jnp
from jax import lax
from jax.sharding import PartitionSpec as P

KVH = 4
HD = 128
SEGL = 32
eps = 1e-05


def normalize_rows(rows, norm_gain):
    values = rows.astype(jnp.float32)
    scale = lax.rsqrt(jnp.mean(values * values, axis=-1, keepdims=True) + eps)
    return (values * scale * norm_gain).astype(jnp.bfloat16)


def segment_pool(seg_keys, seg_values, queries, head_size):
    scores = jnp.einsum(
        "sthd,shd->sth", seg_keys, queries, precision=lax.Precision.HIGHEST
    ) / math.sqrt(head_size)
    scores = scores - jnp.max(scores, axis=1, keepdims=True)
    weights = jnp.exp(scores)
    weights = weights / jnp.sum(weights, axis=1, keepdims=True)
    summary_key = jnp.einsum("sth,sthd->shd", weights, seg_keys, precision=lax.Precision.HIGHEST)
    summary_value = jnp.einsum(
        "sth,sthd->shd", weights, seg_values, precision=lax.Precision.HIGHEST
    )
    return (summary_key, summary_value)


def cross_pool(query_keys, key_all, value_all, live_all, head_size):
    scores = jnp.einsum(
        "jhd,ihd->jhi", query_keys, key_all, precision=lax.Precision.HIGHEST
    ) / math.sqrt(head_size)
    scores = jnp.where(live_all[None, None, :], scores, -1e30)
    highest = jnp.max(scores, axis=2, keepdims=True)
    weights = jnp.where(live_all[None, None, :], jnp.exp(scores - highest), 0.0)
    total = jnp.sum(weights, axis=2, keepdims=True)
    return jnp.einsum("jhi,ihd->jhd", weights, value_all, precision=lax.Precision.HIGHEST) / total


def project_pair(row_block, pieces):
    return (
        jnp.dot(row_block, pieces[0], preferred_element_type=jnp.float32),
        jnp.dot(row_block, pieces[1], preferred_element_type=jnp.float32),
    )


def local(
    draft_tokens,
    draft_gate,
    draft_up,
    draft_head,
    verifier_rows,
    norm_gain,
    key_weight,
    value_weight,
    pool_query,
    flags,
    owner,
):
    seg_count = flags.shape[0]
    gate, upward = project_pair(
        draft_tokens,
        (
            lax.all_gather(draft_gate, "fsdp", axis=0, tiled=True),
            lax.all_gather(draft_up, "fsdp", axis=0, tiled=True),
        ),
    )
    partial_scores = jnp.sum(jax.nn.silu(gate) * upward * draft_head[None, :], axis=1)
    own_scores = lax.psum_scatter(partial_scores, "seq", scatter_dimension=0, tiled=True)
    draft_score = jnp.mean(own_scores.reshape(seg_count, SEGL), axis=1)
    normed = normalize_rows(verifier_rows, norm_gain)
    seg_keys, seg_values = project_pair(
        normed,
        (
            lax.all_gather(key_weight, "fsdp", axis=0, tiled=True),
            lax.all_gather(value_weight, "fsdp", axis=0, tiled=True),
        ),
    )
    lane_pick = (
        owner[:, None] == jnp.arange(pool_query.shape[0], dtype=jnp.int32)[None, :]
    ).astype(jnp.float32)
    queries = jnp.einsum("sc,chd->shd", lane_pick, pool_query, precision=lax.Precision.HIGHEST)
    summary_key, summary_value = segment_pool(
        seg_keys.reshape(seg_count, SEGL, KVH, HD),
        seg_values.reshape(seg_count, SEGL, KVH, HD),
        queries,
        HD,
    )
    live_own = flags.astype(jnp.float32)
    key_all, value_all, live_all = (
        lax.all_gather(summary_key.reshape(seg_count, KVH * HD), "seq", axis=0, tiled=True),
        lax.all_gather(summary_value.reshape(seg_count, KVH * HD), "seq", axis=0, tiled=True),
        lax.all_gather(live_own, "seq", axis=0, tiled=True),
    )
    pooled = cross_pool(
        summary_key,
        key_all.reshape(-1, KVH, HD),
        value_all.reshape(-1, KVH, HD),
        live_all > 0.5,
        HD,
    )
    own_pooled = pooled.reshape(seg_count, KVH * HD)
    verdict = jnp.where(
        flags[:, None] == 1, jax.nn.sigmoid(draft_score)[:, None] * own_pooled, 0.0
    ).astype(jnp.bfloat16)
    return (draft_score, verdict)


def solution(mesh):
    return jax.shard_map(
        local,
        mesh=mesh,
        in_specs=(
            P("fsdp", None),
            P("fsdp", "seq"),
            P("fsdp", "seq"),
            P("seq"),
            P(("fsdp", "seq"), None),
            P(),
            P("fsdp", None),
            P("fsdp", None),
            P(),
            P(("fsdp", "seq")),
            P(("fsdp", "seq")),
        ),
        out_specs=(P(("fsdp", "seq")), P(("fsdp", "seq"), None)),
        check_vma=False,
    )
```

profile of v0, /device:TPU:0, one launch (start us, length us, event | category | flops | bytes accessed | tf_op | source)
XLA Modules:
  0.0 243.5 jit_solution(6076633560900266448)
XLA Ops:
  7.2 0.0 copy-start
  7.2 0.0 all-gather.5.cloned.1.call-start
  7.2 0.7 all-gather.5.cloned.1.call-update
  7.9 0.0 all-gather.7.cloned.1.call-start
  8.0 0.7 all-gather.7.cloned.1.call-update
  8.7 0.0 all-gather.9.cloned.1.call-start
  8.7 0.7 all-gather.9.cloned.1.call-update
  9.4 0.0 all-gather.11.cloned.1.call-start
  9.4 0.5 all-gather.11.cloned.1.call-update
  10.0 1.3 fusion.44
  12.6 0.0 copy-done
  12.6 0.9 convolution_bitcast_fusion.1
  13.5 0.7 broadcast_compare_fusion.1
  14.1 0.7 convert_dynamic-update-slice_fusion
  14.9 3.1 %fusion.1 = f32[256]{0:T(256)S(1)} fusion(bf16[256,8192]{1,0:T(8,128)(2,1)} %param.15), kind=kLoop, calls=%fused_computation.3 | loop fusion | flops 6291200 | bytes 4195328 | tf_op jit(solution)/shard_map/reduce_sum | solution.py:15
  18.0 0.0 copy-start.2
  18.0 41.0 %all-gather.5.cloned.1.call-done = bf16[2048,1024]{1,0:T(8,128)(2,1)} async-done(((bf16[64,1024]{1,0:T(8,128)(2,1)}), bf16[2048,1024]{1,0:T(8,128)(2,1)}) %all-gather.5.cloned.1.call-update) | async-done | bytes 4194320 | tf_op jit(solution)/shard_map/all_gather | solution.py:68
  59.0 10.0 %fusion.47 = f32[1024,1024]{0,1:T(8,128)} fusion(bf16[1024,2048]{1,0:T(8,128)(2,1)} %param.11, bf16[2048,1024]{1,0:T(8,128)(2,1)} %all-gather.5.cloned.1.call-done), kind=kOutput, calls=%fused_computation.63 | convolution fusion | flops 4294967296 | bytes 12582912 | tf_op jit(solution)/shard_map/dot_general | solution.py:46
  69.0 0.0 copy-start.1
  69.0 37.8 %all-gather.7.cloned.1.call-done = bf16[2048,1024]{1,0:T(8,128)(2,1)} async-done(((bf16[64,1024]{1,0:T(8,128)(2,1)}), bf16[2048,1024]{1,0:T(8,128)(2,1)}) %all-gather.7.cloned.1.call-update) | async-done | bytes 4194320 | tf_op jit(solution)/shard_map/all_gather | solution.py:69
  106.7 0.0 copy-done.2
  106.7 10.1 %multiply_reduce_fusion = f32[1024]{0:T(1024)S(1)} fusion(f32[1024,1024]{0,1:T(8,128)} %fusion.47, bf16[1024,2048]{1,0:T(8,128)(2,1)} %param.11, bf16[2048,1024]{1,0:T(8,128)(2,1)} %all-gather.7.cloned.1.call-done, f32[1024]{0:T(1024)S(1)} %copy-done.2), kind=kOutput, calls=%fused_computation.6 | convolution fusion | flops 4302306304 | bytes 12591104 | tf_op jit(solution)/shard_map/dot_general | solution.py:47
  116.9 10.7 %all-reduce.2 = (f32[1024]{0:T(1024)S(1)}, f32[32]{0:T(128)S(1)}) all-reduce(f32[1024]{0:T(1024)S(1)} %multiply_reduce_fusion, f32[32]{0:T(128)S(1)} %convert_dynamic-update-slice_fusion), channel_id=2, replica_groups=mesh['fsdp'=32,'seq'=4] {'seq'}, use_global_device_ids=true, to_apply=%region_1.2.clone | all-reduce | flops 1056 | bytes 8448
  127.6 0.1 dynamic-slice.2
  127.6 0.1 reshape.53
  127.7 0.1 reduce_sum.46
  127.9 0.5 add_divide_fusion
  128.4 32.8 %all-gather.9.cloned.1.call-done = bf16[8192,512]{1,0:T(8,128)(2,1)} async-done(((bf16[256,512]{1,0:T(8,128)(2,1)}), bf16[8192,512]{1,0:T(8,128)(2,1)}) %all-gather.9.cloned.1.call-update) | async-done | bytes 8388624 | tf_op jit(solution)/shard_map/all_gather | solution.py:79
  161.2 0.0 copy-done.1
  161.2 7.0 %fusion.6 = f32[256,512]{1,0:T(8,128)S(1)} fusion(bf16[8192,512]{1,0:T(8,128)(2,1)} %all-gather.9.cloned.1.call-done, bf16[256,8192]{1,0:T(8,128)(2,1)} %param.15, f32[8192]{0:T(1024)S(1)} %copy-done.1, f32[256]{0:T(256)S(1)} %add_rsqrt_fusion), kind=kOutput, calls=%fused_computation.8 | convolution fusion | flops 2155872256 | bytes 13140992 | tf_op jit(solution)/shard_map/dot_general | solution.py:46
  168.2 0.2 reshape.54
  168.4 0.9 fusion.21
  169.3 0.7 fusion.45
  170.0 0.1 divide_bitcast_fusion
  170.1 0.5 fusion.19
  170.6 12.2 %all_gather.27 = f32[32,512]{1,0:T(8,128)S(1)} all-gather(f32[8,512]{1,0:T(8,128)S(1)} %bitcast.83), channel_id=1, replica_groups=mesh['fsdp'=32,'seq'=4] {'seq'}, dimensions={0}, use_global_device_ids=true | all-gather | bytes 81920 | tf_op jit(solution)/shard_map/all_gather | solution.py:95
  182.8 32.9 %all-gather.11.cloned.1.call-done = bf16[8192,512]{1,0:T(8,128)(2,1)} async-done(((bf16[256,512]{1,0:T(8,128)(2,1)}), bf16[8192,512]{1,0:T(8,128)(2,1)}) %all-gather.11.cloned.1.call-update) | async-done | bytes 8388624 | tf_op jit(solution)/shard_map/all_gather | solution.py:80
  215.7 7.0 %fusion.4 = f32[256,512]{1,0:T(8,128)S(1)} fusion(bf16[8192,512]{1,0:T(8,128)(2,1)} %all-gather.11.cloned.1.call-done, bf16[256,8192]{1,0:T(8,128)(2,1)} %param.15, f32[8192]{0:T(1024)S(1)} %copy-done.1, f32[256]{0:T(256)S(1)} %add_rsqrt_fusion), kind=kOutput, calls=%fused_computation.7 | convolution fusion | flops 2155872256 | bytes 13140992 | tf_op jit(solution)/shard_map/dot_general | solution.py:47
  222.7 0.2 reshape.55
  222.9 0.5 fusion.17
  223.5 12.2 %all_gather.25 = f32[32,512]{1,0:T(8,128)S(1)} all-gather(f32[8,512]{1,0:T(8,128)S(1)} %bitcast.82), channel_id=1, replica_groups=mesh['fsdp'=32,'seq'=4] {'seq'}, dimensions={0}, use_global_device_ids=true | all-gather | bytes 81920 | tf_op jit(solution)/shard_map/all_gather | solution.py:96
  235.6 0.3 fusion.46
  235.9 0.2 fusion.31
  236.1 0.9 fusion.16
  (5 shorter events, 0.0 us)
Async XLA Ops:
  7.2 5.4 %copy-start = (f32[4,4,128]{2,1,0:T(4,128)S(1)}, f32[4,4,128]{2,1,0:T(4,128)}, u32[]{:S(2)}) copy-start(f32[4,4,128]{2,1,0:T(4,128)} %param.19) | copy-start | bytes 24580
  7.2 51.8 %all-gather.5.cloned.1.call-start = ((), (), s32[]{:S(2)}) async-start(), calls=%async_computation | async-start | bytes 4325376 | tf_op jit(solution)/shard_map/all_gather | solution.py:68
  7.9 98.8 %all-gather.7.cloned.1.call-start = ((), (), s32[]{:S(2)}) async-start(), calls=%async_computation.1 | async-start | bytes 4325376 | tf_op jit(solution)/shard_map/all_gather | solution.py:69
  8.7 152.5 %all-gather.9.cloned.1.call-start = ((), (), s32[]{:S(2)}) async-start(), calls=%async_computation.2 | async-start | bytes 8650752 | tf_op jit(solution)/shard_map/all_gather | solution.py:79
  9.4 206.3 %all-gather.11.cloned.1.call-start = ((), (), s32[]{:S(2)}) async-start(), calls=%async_computation.3 | async-start | bytes 8650752 | tf_op jit(solution)/shard_map/all_gather | solution.py:80
  18.0 88.7 %copy-start.2 = (f32[1024]{0:T(1024)S(1)}, f32[1024]{0:T(1024)}, u32[]{:S(2)}) copy-start(f32[1024]{0:T(1024)} %param.14) | copy-start | bytes 12292
  69.0 92.2 %copy-start.1 = (f32[8192]{0:T(1024)S(1)}, f32[8192]{0:T(1024)}, u32[]{:S(2)}) copy-start(f32[8192]{0:T(1024)} %param.16) | copy-start | bytes 98308
Sparse Core Ops, SparseCore 0:
  10.2 48.6 all-gather.4
  61.2 45.4 all-gather.6
  109.0 52.1 all-gather.8
  163.3 52.3 all-gather.10
where the time goes:
time: 244 us; the launch traced here: 243 us
  waiting for transfers between devices  147 us (60%)
  matrix products  38.2 us (16%)
  blocking collectives  35 us (14%)
  between operations  15.2 us (6%)
  other arithmetic  6.1 us (2%)
    all_gather x1, waiting for transfers between devices, local(): lax.all_gather(draft_gate, 'fsdp', axis=0, tiled=True)  41 us
    all_gather x1, waiting for transfers between devices, local(): lax.all_gather(draft_up, 'fsdp', axis=0, tiled=True)  37.8 us
    all_gather x1, waiting for transfers between devices, local(): lax.all_gather(value_weight, 'fsdp', axis=0, tiled=True)  32.9 us
    all_gather x1, waiting for transfers between devices, local(): lax.all_gather(key_weight, 'fsdp', axis=0, tiled=True)  32.8 us
    dot_general x2, matrix products, project_pair(): jnp.dot(row_block, pieces[1], preferred_element_type=jnp.float32)  17.2 us
    dot_general x2, matrix products, project_pair(): jnp.dot(row_block, pieces[0], preferred_element_type=jnp.float32)  17 us
    all_gather x1, blocking collectives, local(): lax.all_gather(summary_value.reshape(seg_count, KVH * HD), 'seq', axis=0,...  12.2 us
    all_gather x1, blocking collectives, local(): lax.all_gather(summary_key.reshape(seg_count, KVH * HD), 'seq', axis=0, t...  12.2 us
  transfers between devices with their start and end apart: 4, of which 4 were waited for; matrix products, arithmetic and copies ran while one was open for 15% of the time, Pallas kernels for 0%

commit v1 on v0

--- a/solution.py
+++ b/solution.py
@@ -76,7 +76,10 @@
     seg_keys, seg_values = project_pair(
         normed,
         (
-            lax.all_gather(key_weight, "fsdp", axis=0, tiled=True),
+            jnp.concatenate(
+                lax.all_to_all(jnp.stack([key_weight] * lax.axis_size("fsdp")), "fsdp", 0, 0),
+                axis=0,
+            ),
             lax.all_gather(value_weight, "fsdp", axis=0, tiled=True),
         ),
     )

time: 244 us -> 264 us (1.082)
  local copies, waits for them, and re-layouts: 1.87 us -> 29.6 us
  waiting for transfers between devices: 147 us -> 130 us
  starting transfers between devices: 0.15 us -> 8.82 us
    all_to_all x0 -> x1, waiting for transfers between devices: none -> 104 us  [local(): lax.all_to_all(jnp.stack([key_weight] * lax.axis_size('fsdp')), 'fsdp', 0...]
    all_gather x1, waiting for transfers between devices: 41 us -> 0.02 us  [local(): lax.all_gather(draft_gate, 'fsdp', axis=0, tiled=True)]
    all_gather x1, waiting for transfers between devices: 37.8 us -> 3.35 us  [local(): lax.all_gather(draft_up, 'fsdp', axis=0, tiled=True)]
    all_gather x1 -> x0, waiting for transfers between devices: 32.8 us -> none  [local(): lax.all_gather(key_weight, 'fsdp', axis=0, tiled=True)]
    all_gather x1, waiting for transfers between devices: 32.9 us -> 20.4 us  [local(): lax.all_gather(value_weight, 'fsdp', axis=0, tiled=True)]
    all_to_all x0 -> x1, local copies, waits for them, and re-layouts: none -> 12 us  [local(): lax.all_to_all(jnp.stack([key_weight] * lax.axis_size('fsdp')), 'fsdp', 0...]
    dot_general x0 -> x1, local copies, waits for them, and re-layouts: none -> 11.4 us  [project_pair(): jnp.dot(row_block, pieces[0], preferred_element_type=jnp.float32)]
    all_to_all x0 -> x1, starting transfers between devices: none -> 8.71 us  [local(): lax.all_to_all(jnp.stack([key_weight] * lax.axis_size('fsdp')), 'fsdp', 0...]
  transfers between devices with their start and end apart: 4 -> 4, of which waited for: 4 -> 3; matrix products, arithmetic and copies ran while one was open for 15% -> 25% of each run, Pallas kernels for 0% -> 0%
where the time goes in v1:
time: 264 us; the launch traced here: 263 us
  waiting for transfers between devices  130 us (49%)
  matrix products  36.7 us (14%)
  blocking collectives  34.7 us (13%)
  local copies, waits for them, and re-layouts  29.6 us (11%)
  between operations  15.2 us (6%)
  starting transfers between devices  8.82 us (3%)
  other arithmetic  8.23 us (3%)
    all_to_all x1, waiting for transfers between devices, local(): lax.all_to_all(jnp.stack([key_weight] * lax.axis_size('fsdp')), 'fsdp', 0...  104 us
    all_gather x1, waiting for transfers between devices, local(): lax.all_gather(value_weight, 'fsdp', axis=0, tiled=True)  20.4 us
    dot_general x2, matrix products, project_pair(): jnp.dot(row_block, pieces[1], preferred_element_type=jnp.float32)  17.1 us
    dot_general x2, matrix products, project_pair(): jnp.dot(row_block, pieces[0], preferred_element_type=jnp.float32)  16.2 us
    all_gather x1, blocking collectives, local(): lax.all_gather(summary_value.reshape(seg_count, KVH * HD), 'seq', axis=0,...  12.2 us
    all_gather x1, blocking collectives, local(): lax.all_gather(summary_key.reshape(seg_count, KVH * HD), 'seq', axis=0, t...  12.1 us
    all_to_all x1, local copies, waits for them, and re-layouts, local(): lax.all_to_all(jnp.stack([key_weight] * lax.axis_size('fsdp')), 'fsdp', 0...  12 us
    dot_general x1, local copies, waits for them, and re-layouts, project_pair(): jnp.dot(row_block, pieces[0], preferred_element_type=jnp.float32)  11.4 us
  transfers between devices with their start and end apart: 4, of which 3 were waited for; matrix products, arithmetic and copies ran while one was open for 25% of the time, Pallas kernels for 0%

profile of v1, /device:TPU:0, one launch (start us, length us, event | category | flops | bytes accessed | tf_op | source)
XLA Modules:
  0.0 262.9 jit_solution(11077858879582267644)
XLA Ops:
  7.2 0.0 copy-start
  7.2 0.0 all-gather.4.cloned.1.call-start
  7.2 0.7 all-gather.4.cloned.1.call-update
  7.9 0.0 all-gather.6.cloned.1.call-start
  8.0 0.7 all-gather.6.cloned.1.call-update
  8.7 0.0 all-gather.8.cloned.1.call-start
  8.7 0.7 all-gather.8.cloned.1.call-update
  9.4 1.1 copy.28
  10.5 4.2 %stack.2 = bf16[32,256,512]{1,2,0:T(8,128)(2,1)} broadcast(bf16[256,512]{0,1:T(8,128)(2,1)S(1)} %copy.28), dimensions={1,2} | broadcast | bytes 8650752 | tf_op jit(solution)/shard_map/stack | solution.py:80
  14.7 0.0 copy-start.4
  14.7 0.0 copy-start.5
  14.7 0.0 copy-start.7
  14.7 8.7 %all-to-all-start = ((bf16[32,256,512]{1,2,0:T(8,128)(2,1)}), bf16[32,256,512]{1,2,0:T(8,128)(2,1)}, u32[]{:S(2)}, u32[]{:S(2)}) async-start(bf16[32,256,512]{1,2,0:T(8,128)(2,1)} %stack.2), calls=%async_computation | async-start | bytes 16777216 | tf_op jit(solution)/shard_map/all_to_all | solution.py:80
  23.4 0.0 copy-start.3
  23.4 0.0 copy-done.4
  23.4 0.6 fusion.38
  25.3 0.0 copy-done
  25.3 0.0 copy-done.5
  25.3 0.0 copy-start.2
  25.3 0.2 convolution_bitcast_fusion.1
  25.5 0.0 copy-done.7
  25.5 0.1 convert_dynamic-update-slice_fusion
  25.6 3.3 %fusion.1 = f32[256]{0:T(256)S(1)} fusion(bf16[256,8192]{1,0:T(8,128)(2,1)} %param.15), kind=kLoop, calls=%fused_computation.3 | loop fusion | flops 6291200 | bytes 4195328 | tf_op jit(solution)/shard_map/reduce_sum | solution.py:15
  28.9 0.0 copy-done.3
  28.9 0.0 copy-done.2
  28.9 3.2 %fusion.3 = bf16[256,8192]{1,0:T(8,128)(2,1)} fusion(bf16[256,8192]{1,0:T(8,128)(2,1)S(1)} %copy-done.2, f32[8192]{0:T(1024)S(1)} %copy-done.3, f32[256]{0:T(256)S(1)} %add_rsqrt_fusion), kind=kLoop, calls=%fused_computation.5 | loop fusion | flops 8388608 | bytes 8422400 | tf_op jit(solution)/shard_map/convert_element_type | solution.py:16
  32.2 103.9 %all-to-all-done = bf16[32,256,512]{1,2,0:T(8,128)(2,1)} async-done(((bf16[32,256,512]{1,2,0:T(8,128)(2,1)}), bf16[32,256,512]{1,2,0:T(8,128)(2,1)}, u32[]{:S(2)}, u32[]{:S(2)}) %all-to-all-start) | async-done | bytes 8388640 | tf_op jit(solution)/shard_map/all_to_all | solution.py:80
  136.0 12.0 %copy.29 = bf16[32,256,512]{2,1,0:T(8,128)(2,1)} copy(bf16[32,256,512]{1,2,0:T(8,128)(2,1)} %all-to-all-done) | data formatting | bytes 16777216 | tf_op jit(solution)/shard_map/all_to_all | solution.py:80
  148.0 11.4 %copy.30 = bf16[512,8192]{1,0:T(8,128)(2,1)} copy(bf16[512,8192]{0,1:T(8,128)(2,1)} %bitcast.97) | data formatting | bytes 16777216 | tf_op jit(solution)/shard_map/dot_general | solution.py:46
  159.4 6.1 %fusion.42 = f32[8,32,4,128]{3,1,2,0:T(8,128)S(1)} fusion(bf16[8,32,8192,1]{2,1,3,0:T(8,128)(2,1)} %bitcast.99, bf16[4,128,8192,1]{2,1,0,3:T(8,128)(2,1)} %bitcast.98), kind=kOutput, calls=%fused_computation.60 | convolution fusion | flops 2147483648 | bytes 13107200 | tf_op jit(solution)/shard_map/dot_general | solution.py:46
  165.5 0.9 fusion.21
  166.4 0.7 fusion.39
  167.1 0.1 divide_bitcast_fusion
  167.2 0.5 fusion.25
  167.8 0.0 copy-start.6
  167.8 0.0 all-gather.4.cloned.1.call-done
  167.8 10.1 %fusion.41 = f32[1024,1024]{0,1:T(8,128)} fusion(bf16[1024,2048]{1,0:T(8,128)(2,1)} %param.11, bf16[2048,1024]{1,0:T(8,128)(2,1)} %all-gather.4.cloned.1.call-done), kind=kOutput, calls=%fused_computation.59 | convolution fusion | flops 4294967296 | bytes 12582912 | tf_op jit(solution)/shard_map/dot_general | solution.py:46
  177.9 3.3 %all-gather.6.cloned.1.call-done = bf16[2048,1024]{1,0:T(8,128)(2,1)} async-done(((bf16[64,1024]{1,0:T(8,128)(2,1)}), bf16[2048,1024]{1,0:T(8,128)(2,1)}) %all-gather.6.cloned.1.call-update) | async-done | bytes 4194320 | tf_op jit(solution)/shard_map/all_gather | solution.py:69
  181.3 0.0 copy-done.6
  181.3 10.1 %multiply_reduce_fusion = f32[1024]{0:T(1024)S(1)} fusion(f32[1024,1024]{0,1:T(8,128)} %fusion.41, bf16[1024,2048]{1,0:T(8,128)(2,1)} %param.11, bf16[2048,1024]{1,0:T(8,128)(2,1)} %all-gather.6.cloned.1.call-done, f32[1024]{0:T(1024)S(1)} %copy-done.6), kind=kOutput, calls=%fused_computation.6 | convolution fusion | flops 4302306304 | bytes 12591104 | tf_op jit(solution)/shard_map/dot_general | solution.py:47
  191.4 10.4 %all-reduce.2 = (f32[1024]{0:T(1024)S(1)}, f32[32]{0:T(128)S(1)}) all-reduce(f32[1024]{0:T(1024)S(1)} %multiply_reduce_fusion, f32[32]{0:T(128)S(1)} %convert_dynamic-update-slice_fusion), channel_id=2, replica_groups=mesh['fsdp'=32,'seq'=4] {'seq'}, use_global_device_ids=true, to_apply=%region_1.2.clone | all-reduce | flops 1056 | bytes 8448
  201.8 0.1 dynamic-slice.2
  201.9 0.1 reshape.58
  202.0 0.1 reduce_sum.46
  202.1 12.1 %all_gather.23 = f32[32,512]{1,0:T(8,128)S(1)} all-gather(f32[8,512]{1,0:T(8,128)S(1)} %bitcast.100), channel_id=1, replica_groups=mesh['fsdp'=32,'seq'=4] {'seq'}, dimensions={0}, use_global_device_ids=true | all-gather | bytes 81920 | tf_op jit(solution)/shard_map/all_gather | solution.py:98
  214.2 0.3 fusion.40
  214.5 0.2 fusion.24
  214.7 0.5 add_divide_fusion
  215.2 20.4 %all-gather.8.cloned.1.call-done = bf16[8192,512]{1,0:T(8,128)(2,1)} async-done(((bf16[256,512]{1,0:T(8,128)(2,1)}), bf16[8192,512]{1,0:T(8,128)(2,1)}) %all-gather.8.cloned.1.call-update) | async-done | bytes 8388624 | tf_op jit(solution)/shard_map/all_gather | solution.py:83
  235.6 0.0 copy-start.1
  235.6 7.0 %fusion.43 = f32[256,512]{1,0:T(8,128)S(1)} fusion(bf16[256,8192]{1,0:T(8,128)(2,1)} %fusion.3, bf16[8192,512]{1,0:T(8,128)(2,1)} %all-gather.8.cloned.1.call-done), kind=kOutput, calls=%fused_computation.61 | convolution fusion | flops 2147483648 | bytes 13107200 | tf_op jit(solution)/shard_map/dot_general | solution.py:47
  242.6 0.2 reshape.60
  242.8 0.5 fusion.13
  243.3 12.2 %all_gather.21 = f32[32,512]{1,0:T(8,128)S(1)} all-gather(f32[8,512]{1,0:T(8,128)S(1)} %bitcast.101), channel_id=1, replica_groups=mesh['fsdp'=32,'seq'=4] {'seq'}, dimensions={0}, use_global_device_ids=true | all-gather | bytes 81920 | tf_op jit(solution)/shard_map/all_gather | solution.py:99
  255.5 0.8 fusion.12
  256.3 0.0 copy-done.1
  (6 shorter events, 0.0 us)
Async XLA Ops:
  7.2 18.1 %copy-start = (f32[4,4,128]{2,1,0:T(4,128)S(1)}, f32[4,4,128]{2,1,0:T(4,128)}, u32[]{:S(2)}) copy-start(f32[4,4,128]{2,1,0:T(4,128)} %param.19) | copy-start | bytes 24580
  7.2 160.6 %all-gather.4.cloned.1.call-start = ((), (), s32[]{:S(2)}) async-start(), calls=%async_computation.1 | async-start | bytes 4325376 | tf_op jit(solution)/shard_map/all_gather | solution.py:68
  7.9 173.4 %all-gather.6.cloned.1.call-start = ((), (), s32[]{:S(2)}) async-start(), calls=%async_computation.2 | async-start | bytes 4325376 | tf_op jit(solution)/shard_map/all_gather | solution.py:69
  8.7 226.9 %all-gather.8.cloned.1.call-start = ((), (), s32[]{:S(2)}) async-start(), calls=%async_computation.3 | async-start | bytes 8650752 | tf_op jit(solution)/shard_map/all_gather | solution.py:83
  14.7 8.7 %copy-start.4 = (u32[128]{0:T(128)S(1)}, u32[128]{0:T(128)}, u32[]{:S(2)}) copy-start(u32[128]{0:T(128)} %constant.31) | copy-start | bytes 1540
  14.7 10.6 %copy-start.5 = (s32[8]{0:T(128)S(1)}, s32[8]{0:T(128)}, u32[]{:S(2)}) copy-start(s32[8]{0:T(128)} %param.21) | copy-start | bytes 100
  14.7 10.9 %copy-start.7 = (s32[8]{0:T(128)S(1)}, s32[8]{0:T(128)}, u32[]{:S(2)}) copy-start(s32[8]{0:T(128)} %param.20) | copy-start | bytes 100
  14.7 121.4 %all-to-all-start = ((bf16[32,256,512]{1,2,0:T(8,128)(2,1)}), bf16[32,256,512]{1,2,0:T(8,128)(2,1)}, u32[]{:S(2)}, u32[]{:S(2)}) async-start(bf16[32,256,512]{1,2,0:T(8,128)(2,1)} %stack.2), calls=%async_computation | async-start | bytes 16777216 | tf_op jit(solution)/shard_map/all_to_all | solution.py:80
  23.4 5.6 %copy-start.3 = (f32[8192]{0:T(1024)S(1)}, f32[8192]{0:T(1024)}, u32[]{:S(2)}) copy-start(f32[8192]{0:T(1024)} %param.16) | copy-start | bytes 98308
  25.3 3.6 %copy-start.2 = (bf16[256,8192]{1,0:T(8,128)(2,1)S(1)}, bf16[256,8192]{1,0:T(8,128)(2,1)}, u32[]{:S(2)}) copy-start(bf16[256,8192]{1,0:T(8,128)(2,1)} %param.15) | copy-start | bytes 12582916
  167.8 13.5 %copy-start.6 = (f32[1024]{0:T(1024)S(1)}, f32[1024]{0:T(1024)}, u32[]{:S(2)}) copy-start(f32[1024]{0:T(1024)} %param.14) | copy-start | bytes 12292
  235.6 20.7 %copy-start.1 = (f32[4,4,128]{2,1,0:T(4,128)S(1)}, f32[4,4,128]{2,1,0:T(4,128)}, u32[]{:S(2)}) copy-start(f32[4,4,128]{2,1,0:T(4,128)} %param.19) | copy-start | bytes 24580
Sparse Core Ops, SparseCore 0:
  10.3 116.5 all-gather.3
  129.1 52.0 all-gather.5
  183.5 52.0 all-gather.7
